TPU v7x, 256 devices: a whole 4x4x8 slice. The times are simulated.
256 devices in a mesh: dom: 64 (over z, x, core), sub: 4 (over y).
Axes of the slice: x: 4, y: 4, z: 8, core: 2. Of those that a mesh axis runs over, the one named last changes fastest.
Arguments:
- excitation: bfloat16 [64, 1536, 64], P('dom', 'sub'), may hold values from -6 to 6
- local_inverse: bfloat16 [64, 1536, 1536], P('dom', 'sub'), as said below
- aggregation: bfloat16 [64, 1024, 1536], P('dom', None, 'sub'), may hold values from -0.15625 to 0.15625
- disaggregation: bfloat16 [64, 1536, 1024], P('dom', 'sub'), may hold values from -0.1875 to 0.1875
- translation: float32 [64, 6, 2, 512], P('dom'), may hold values from -1.5 to 1.5
- partners: int32 [64, 6], P('dom'), may hold values from 0 to 63, as said below
- list_counts: int32 [64], P('dom'), may hold values from 2 to 6
- sweep_order: int32 [64], replicated, may hold values from 0 to 63, as said below
Outputs:
- currents: float32 [64, 1536, 64], P('dom', 'sub')
Inputs may be any that keep to these rules, and one draw needn't show every extreme that they name: `partners`: row d names 6 different subdomains, none equal to d; only its first list_counts[d] slots are used. `local_inverse`: each subdomain's matrix is the identity plus independent entries of spread 0.6 / sqrt(1536). `sweep_order`: every subdomain has a position of its own.
All inputs are finite; a program needn't handle non-finite values.
Results may differ from a plain program's by a relative error of at most 0.03.
Values may be sent and summed in bfloat16 or wider, within the bound.
No kernel may reach another device: no remote copies, remote signals or barrier semaphores. Data moves between devices by JAX's collectives and lax.ppermute only.
A program may use at most 64 MiB of HBM per device.

v0:
```python
import jax
import jax.numpy as jnp
from jax import lax
from jax.sharding import Mesh
from jax.sharding import PartitionSpec as P

SEGMENTS = 8
CORES = 2
CONTRACT_FIRST = (((0,), (1,)), ((), ()))
CONTRACT_LAST = (((1,), (1,)), ((), ()))
DOM = ("zx", "core")


def rotate(real_weight, imag_weight, pattern):
    samples = real_weight.shape[-1]
    values = pattern.astype(jnp.float32)
    real_part = values[..., :samples]
    imag_part = values[..., samples:]
    return jnp.concatenate(
        [
            real_weight * real_part - imag_weight * imag_part,
            real_weight * imag_part + imag_weight * real_part,
        ],
        axis=-1,
    )


def share_slots(slots, chips):
    shape = slots.shape
    swap = [(0, 1), (1, 0)]
    slots = slots + lax.ppermute(slots, "core", swap)
    core = lax.axis_index("core")
    halves = slots.reshape(CORES, -1)
    mine = lax.dynamic_index_in_dim(halves, core, 0, keepdims=False).reshape(chips, -1)
    pieces = lax.all_to_all(mine, "zx", 0, 0, tiled=True)
    total = jnp.sum(pieces, axis=0, keepdims=True)
    spread = jnp.broadcast_to(total, (chips, total.shape[1]))
    gathered = lax.all_to_all(spread, "zx", 0, 0, tiled=True).reshape(-1)
    other = lax.ppermute(gathered, "core", swap)
    whole = jnp.where(
        core == 0, jnp.concatenate([gathered, other]), jnp.concatenate([other, gathered])
    )
    return whole.reshape(shape)


def local(
    excitation,
    local_inverse,
    aggregation,
    disaggregation,
    translation,
    partners,
    list_counts,
    sweep_order,
):
    chips = lax.axis_size("zx")
    excite_rows = excitation[0]
    inverse_rows = local_inverse[0]
    agg_columns = aggregation[0]
    disagg_rows = disaggregation[0]
    trans_rows = translation[0]
    partner_row = partners[0]

    def apply_inverse(shard_rows):
        return jnp.dot(inverse_rows, shard_rows, preferred_element_type=jnp.float32)

    solved = apply_inverse(lax.all_gather(excite_rows, "sub", axis=0, tiled=True))
    solved_half = solved.astype(jnp.bfloat16)
    incident = lax.psum_scatter(
        lax.dot_general(
            solved_half, agg_columns, CONTRACT_FIRST, preferred_element_type=jnp.float32
        ).astype(jnp.bfloat16),
        "sub",
        scatter_dimension=0,
        tiled=True,
    ).astype(jnp.float32)
    spread = apply_inverse(lax.all_gather(disagg_rows, "sub", axis=0, tiled=True))
    spread_half = spread.astype(jnp.bfloat16)
    partial_map = lax.dot_general(
        spread_half, agg_columns, CONTRACT_FIRST, preferred_element_type=jnp.float32
    )
    coupling = lax.psum(partial_map.astype(jnp.bfloat16), "sub")
    domains = sweep_order.shape[0]
    members = domains // SEGMENTS
    segment_of = sweep_order * SEGMENTS // domains
    own_index = lax.axis_index("zx") * CORES + lax.axis_index("core")
    my_segment = segment_of[own_index]
    my_slot = sweep_order[own_index] - my_segment * members
    slot_ids = jnp.arange(members, dtype=jnp.int32)
    slot_live = jnp.arange(partner_row.shape[0], dtype=jnp.int32) < list_counts[0]
    partner_pos = sweep_order[partner_row]
    partner_segment = partner_pos * SEGMENTS // domains
    partner_slot = partner_pos - partner_segment * members
    incoming = jnp.zeros(incident.shape, jnp.float32)
    for segment_k in range(SEGMENTS - 1):
        pattern = (
            incident
            - jnp.dot(incoming.astype(jnp.bfloat16), coupling, preferred_element_type=jnp.float32)
        ).astype(jnp.bfloat16)
        mine = (slot_ids == my_slot) & (my_segment == segment_k)
        slots = jnp.where(mine[:, None, None], pattern[None], jnp.zeros_like(pattern)[None])
        slots = share_slots(slots, chips)
        match = (
            (partner_slot[:, None] == slot_ids[None, :])
            & (partner_segment[:, None] == segment_k)
            & slot_live[:, None]
            & (segment_k < my_segment)
        )
        weights = jnp.sum(
            jnp.where(match[:, :, None, None], trans_rows[:, None, :, :], 0.0), axis=0
        )
        terms = rotate(weights[:, 0][:, None, :], weights[:, 1][:, None, :], slots)
        incoming = incoming + jnp.sum(terms, axis=0)
    fields = lax.all_gather(incoming.astype(jnp.bfloat16), "sub", axis=0, tiled=True)
    currents = solved - lax.dot_general(
        spread_half, fields, CONTRACT_LAST, preferred_element_type=jnp.float32
    )
    return currents[None]


def solution(mesh):
    dom_size, sub_size = mesh.devices.shape
    fine = Mesh(mesh.devices.reshape(dom_size // CORES, CORES, sub_size), ("zx", "core", "sub"))
    in_specs = (
        P(DOM, "sub", None),
        P(DOM, "sub", None),
        P(DOM, None, "sub"),
        P(DOM, "sub", None),
        P(DOM, None, None, None),
        P(DOM, None),
        P(DOM),
        P(),
    )
    out_specs = P(DOM, "sub", None)
    return jax.shard_map(local, mesh=fine, in_specs=in_specs, out_specs=out_specs, check_vma=False)
```

profile of v0, /device:TPU:32, one launch (start us, length us, event | category | flops | bytes accessed | tf_op | source)
XLA Modules:
  0.0 538.5 jit_solution(2973069429768945431)
XLA Ops:
  7.3 12.9 %all-gather = bf16[1,1536,64]{1,2,0:T(8,128)(2,1)S(1)} all-gather(bf16[1,384,64]{1,2,0:T(8,128)(2,1)} %param.8), channel_id=2, replica_groups=mesh['zx'=32,'core'=2,'sub'=4] {'sub'}, dimensions={1}, use_global_device_ids=true | all-gather | bytes 245760 | tf_op jit(solution)/shard_map/all_gather | solution.py:67
  21.9 32.1 %all-gather.4.cloned.1.call-done = bf16[1,1536,1024]{2,1,0:T(8,128)(2,1)} async-done(((bf16[1,384,1024]{2,1,0:T(8,128)(2,1)}), bf16[1,1536,1024]{2,1,0:T(8,128)(2,1)}) %all-gather.4.cloned.1.call-update) | async-done | bytes 3145744 | tf_op jit(solution)/shard_map/all_gather | solution.py:77
  53.9 3.3 fusion.2
  57.3 2.6 convolution_convert_fusion
  63.2 16.4 %reduce-scatter.2.cloned.1.call-done = bf16[16,1024]{1,0:T(8,128)(2,1)} async-done(((bf16[64,1024]{1,0:T(8,128)(2,1)}), bf16[16,1024]{1,0:T(8,128)(2,1)}) %reduce-scatter.2.cloned.1.call-update) | async-done | bytes 32784 | tf_op jit(solution)/shard_map/reduce_scatter | solution.py:69
  79.6 66.1 %all-reduce.2.cloned.1.call-done = bf16[1024,1024]{1,0:T(8,128)(2,1)} async-done(((bf16[1024,1024]{1,0:T(8,128)(2,1)}), bf16[1024,1024]{1,0:T(8,128)(2,1)}) %all-reduce.2.cloned.1.call-update) | async-done | bytes 2097168 | tf_op jit(solution)/shard_map/psum | solution.py:82
  145.7 2.0 fusion.9
  152.5 10.1 %all-to-all-start = ((bf16[32,2,1024]{2,1,0:T(2,128)(2,1)}), bf16[32,2,1024]{2,1,0:T(2,128)(2,1)S(1)}, u32[]{:S(2)}, u32[]{:S(2)}) async-start(bf16[32,2,1024]{2,1,0:T(2,128)(2,1)} %reshape.728), calls=%async_computation.1 | async-start | bytes 262144 | tf_op jit(solution)/shard_map/all_to_all | solution.py:35
  168.0 4.5 all-to-all-done
  175.0 5.3 all-to-all-start.1
  181.2 8.6 %all-to-all-done.1 = bf16[32,2,1024]{2,1,0:T(2,128)(2,1)S(1)} async-done(((bf16[32,2,1024]{2,1,0:T(2,128)(2,1)}), bf16[32,2,1024]{2,1,0:T(2,128)(2,1)S(1)}, u32[]{:S(2)}, u32[]{:S(2)}) %all-to-all-start.1) | async-done | bytes 131104 | tf_op jit(solution)/shard_map/all_to_all | solution.py:38
  190.7 1.7 reduce.14
  193.0 1.3 slice_bitcast_fusion.13
  203.0 1.8 reshape.692
  204.9 1.9 constant_dynamic-slice_fusion.5
  206.8 2.2 reduce.30
  209.8 15.2 %all_to_all.105 = bf16[32,2,1024]{2,1,0:T(2,128)(2,1)S(1)} all-to-all(bf16[32,2,1024]{2,1,0:T(2,128)(2,1)} %reshape.732), channel_id=1, replica_groups=mesh['zx'=32,'core'=2,'sub'=4] {'zx'}, dimensions={0} | all-to-all | bytes 262144 | tf_op jit(solution)/shard_map/all_to_all | solution.py:35
  227.8 2.2 reduce.31
  230.8 14.3 %all_to_all.106 = bf16[32,2,1024]{2,1,0:T(2,128)(2,1)S(1)} all-to-all(bf16[32,2,1024]{2,1,0:T(2,128)(2,1)} %reshape.734), channel_id=1, replica_groups=mesh['zx'=32,'core'=2,'sub'=4] {'zx'}, dimensions={0} | all-to-all | bytes 262144 | tf_op jit(solution)/shard_map/all_to_all | solution.py:38
  245.9 1.7 reduce.16
  248.2 1.3 slice_bitcast_fusion.11
  251.5 1.6 concatenate.111
  258.2 1.8 reshape.694
  260.1 1.9 constant_dynamic-slice_fusion.4
  262.0 2.9 reduce.32
  264.9 1.6 reshape.736
  266.5 15.3 %all_to_all.107 = bf16[32,2,1024]{2,1,0:T(2,128)(2,1)S(1)} all-to-all(bf16[32,2,1024]{2,1,0:T(2,128)(2,1)} %reshape.736), channel_id=1, replica_groups=mesh['zx'=32,'core'=2,'sub'=4] {'zx'}, dimensions={0} | all-to-all | bytes 262144 | tf_op jit(solution)/shard_map/all_to_all | solution.py:35
  284.6 2.2 reduce.33
  287.5 14.3 %all_to_all.108 = bf16[32,2,1024]{2,1,0:T(2,128)(2,1)S(1)} all-to-all(bf16[32,2,1024]{2,1,0:T(2,128)(2,1)} %reshape.738), channel_id=1, replica_groups=mesh['zx'=32,'core'=2,'sub'=4] {'zx'}, dimensions={0} | all-to-all | bytes 262144 | tf_op jit(solution)/shard_map/all_to_all | solution.py:38
  302.6 1.7 reduce.18
  305.2 1.3 slice_bitcast_fusion.9
  308.4 1.6 concatenate.116
  315.2 1.8 reshape.696
  317.0 1.9 constant_dynamic-slice_fusion.3
  318.9 2.9 reduce.34
  321.8 1.6 reshape.740
  323.4 15.3 %all_to_all.109 = bf16[32,2,1024]{2,1,0:T(2,128)(2,1)S(1)} all-to-all(bf16[32,2,1024]{2,1,0:T(2,128)(2,1)} %reshape.740), channel_id=1, replica_groups=mesh['zx'=32,'core'=2,'sub'=4] {'zx'}, dimensions={0} | all-to-all | bytes 262144 | tf_op jit(solution)/shard_map/all_to_all | solution.py:35
  341.5 2.2 reduce.35
  344.5 14.3 %all_to_all.110 = bf16[32,2,1024]{2,1,0:T(2,128)(2,1)S(1)} all-to-all(bf16[32,2,1024]{2,1,0:T(2,128)(2,1)} %reshape.742), channel_id=1, replica_groups=mesh['zx'=32,'core'=2,'sub'=4] {'zx'}, dimensions={0} | all-to-all | bytes 262144 | tf_op jit(solution)/shard_map/all_to_all | solution.py:38
  359.6 1.7 reduce.20
  361.9 1.3 slice_bitcast_fusion.7
  365.2 1.6 concatenate.121
  371.9 1.8 reshape.698
  373.7 1.9 constant_dynamic-slice_fusion.2
  375.7 2.9 reduce.36
  378.5 1.6 reshape.744
  380.2 15.3 %all_to_all.111 = bf16[32,2,1024]{2,1,0:T(2,128)(2,1)S(1)} all-to-all(bf16[32,2,1024]{2,1,0:T(2,128)(2,1)} %reshape.744), channel_id=1, replica_groups=mesh['zx'=32,'core'=2,'sub'=4] {'zx'}, dimensions={0} | all-to-all | bytes 262144 | tf_op jit(solution)/shard_map/all_to_all | solution.py:35
  398.2 2.2 reduce.37
  401.2 14.7 %all_to_all.112 = bf16[32,2,1024]{2,1,0:T(2,128)(2,1)S(1)} all-to-all(bf16[32,2,1024]{2,1,0:T(2,128)(2,1)} %reshape.746), channel_id=1, replica_groups=mesh['zx'=32,'core'=2,'sub'=4] {'zx'}, dimensions={0} | all-to-all | bytes 262144 | tf_op jit(solution)/shard_map/all_to_all | solution.py:38
  416.7 1.7 reduce.22
  419.1 1.3 slice_bitcast_fusion.5
  422.3 1.6 concatenate.126
  429.7 1.8 reshape.700
  431.5 1.9 constant_dynamic-slice_fusion.1
  433.4 2.2 reduce.38
  436.4 15.3 %all_to_all.113 = bf16[32,2,1024]{2,1,0:T(2,128)(2,1)S(1)} all-to-all(bf16[32,2,1024]{2,1,0:T(2,128)(2,1)} %reshape.748), channel_id=1, replica_groups=mesh['zx'=32,'core'=2,'sub'=4] {'zx'}, dimensions={0} | all-to-all | bytes 262144 | tf_op jit(solution)/shard_map/all_to_all | solution.py:35
  454.5 2.2 reduce.39
  457.4 14.3 %all_to_all.114 = bf16[32,2,1024]{2,1,0:T(2,128)(2,1)S(1)} all-to-all(bf16[32,2,1024]{2,1,0:T(2,128)(2,1)} %reshape.750), channel_id=1, replica_groups=mesh['zx'=32,'core'=2,'sub'=4] {'zx'}, dimensions={0} | all-to-all | bytes 262144 | tf_op jit(solution)/shard_map/all_to_all | solution.py:38
  472.6 1.7 reduce.24
  474.9 1.3 slice_bitcast_fusion.3
  478.2 1.6 concatenate.131
  486.1 14.6 %all_to_all.115 = bf16[32,2,1024]{2,1,0:T(2,128)(2,1)S(1)} all-to-all(bf16[32,2,1024]{2,1,0:T(2,128)(2,1)S(1)} %reshape.752), channel_id=1, replica_groups=mesh['zx'=32,'core'=2,'sub'=4] {'zx'}, dimensions={0} | all-to-all | bytes 262144 | tf_op jit(solution)/shard_map/all_to_all | solution.py:35
  502.5 13.7 %all_to_all.116 = bf16[32,2,1024]{2,1,0:T(2,128)(2,1)S(1)} all-to-all(bf16[32,2,1024]{2,1,0:T(2,128)(2,1)S(1)} %reshape.754), channel_id=1, replica_groups=mesh['zx'=32,'core'=2,'sub'=4] {'zx'}, dimensions={0} | all-to-all | bytes 262144 | tf_op jit(solution)/shard_map/all_to_all | solution.py:38
  518.8 12.0 %all_gather.11 = bf16[64,1024]{1,0:T(8,128)(2,1)S(1)} all-gather(bf16[16,1024]{1,0:T(8,128)(2,1)S(1)} %add_convert_fusion), channel_id=1, replica_groups=mesh['zx'=32,'core'=2,'sub'=4] {'sub'}, dimensions={0}, use_global_device_ids=true | all-gather | bytes 163840 | tf_op jit(solution)/shard_map/all_gather | solution.py:114
  (220 shorter events, 86.3 us)
Async XLA Ops:
  6.5 13.7 %copy-start = (bf16[1,384,1536]{2,1,0:T(8,128)(2,1)S(1)}, bf16[1,384,1536]{2,1,0:T(8,128)(2,1)}, u32[]{:S(2)}) copy-start(bf16[1,384,1536]{2,1,0:T(8,128)(2,1)} %param.9) | copy-start | bytes 3538948
  6.5 14.2 %copy-start.6 = (bf16[1,1024,384]{2,1,0:T(8,128)(2,1)S(1)}, bf16[1,1024,384]{2,1,0:T(8,128)(2,1)}, u32[]{:S(2)}) copy-start(bf16[1,1024,384]{2,1,0:T(8,128)(2,1)} %param.10) | copy-start | bytes 2359300
  6.5 47.4 %all-gather.4.cloned.1.call-start = ((), (), s32[]{:S(2)}) async-start(), calls=%async_computation.17 | async-start | bytes 3932160 | tf_op jit(solution)/shard_map/all_gather | solution.py:77
  7.3 72.3 %reduce-scatter.2.cloned.1.call-start = ((), (), s32[]{:S(2)}) async-start(), calls=%async_computation.15 | async-start | bytes 163840 | tf_op jit(solution)/shard_map/reduce_scatter | solution.py:69
  21.8 123.9 %all-reduce.2.cloned.1.call-start = ((), (), s32[]{:S(2)}) async-start(), calls=%async_computation.16 | async-start | bytes 4194304 | tf_op jit(solution)/shard_map/psum | solution.py:82
  57.2 2.7 copy-start.4
  57.2 2.7 copy-start.1
  57.2 5.9 %copy-start.25 = (s32[1,6]{1,0:T(1,128)S(1)}, s32[1,6]{1,0:T(1,128)}, u32[]{:S(2)}) copy-start(s32[1,6]{1,0:T(1,128)} %param.13) | copy-start | bytes 76
  147.8 1.6 collective-permute-start
  148.6 31.8 %copy-start.18 = (f32[1,6,2,512]{3,2,1,0:T(2,128)S(1)}, f32[1,6,2,512]{3,2,1,0:T(2,128)}, u32[]{:S(2)}) copy-start(f32[1,6,2,512]{3,2,1,0:T(2,128)} %param.12) | copy-start | bytes 73732
  152.5 19.9 %all-to-all-start = ((bf16[32,2,1024]{2,1,0:T(2,128)(2,1)}), bf16[32,2,1024]{2,1,0:T(2,128)(2,1)S(1)}, u32[]{:S(2)}, u32[]{:S(2)}) async-start(bf16[32,2,1024]{2,1,0:T(2,128)(2,1)} %reshape.728), calls=%async_computation.1 | async-start | bytes 262144 | tf_op jit(solution)/shard_map/all_to_all | solution.py:35
  175.0 14.8 %all-to-all-start.1 = ((bf16[32,2,1024]{2,1,0:T(2,128)(2,1)}), bf16[32,2,1024]{2,1,0:T(2,128)(2,1)S(1)}, u32[]{:S(2)}, u32[]{:S(2)}) async-start(bf16[32,2,1024]{2,1,0:T(2,128)(2,1)} %reshape.730), calls=%async_computation.2 | async-start | bytes 262144 | tf_op jit(solution)/shard_map/all_to_all | solution.py:38
  181.2 18.6 %copy-start.2 = (bf16[1024,1024]{1,0:T(8,128)(2,1)S(1)}, bf16[1024,1024]{1,0:T(8,128)(2,1)}, u32[]{:S(2)}) copy-start(bf16[1024,1024]{1,0:T(8,128)(2,1)} %all-reduce.2.cloned.1.call-done) | copy-start | bytes 6291460
  181.2 18.6 %copy-start.3 = (bf16[16,1024]{1,0:T(8,128)(2,1)S(1)}, bf16[16,1024]{1,0:T(8,128)(2,1)}, u32[]{:S(2)}) copy-start(bf16[16,1024]{1,0:T(8,128)(2,1)} %reduce-scatter.2.cloned.1.call-done) | copy-start | bytes 98308
  193.0 3.3 collective-permute-start.1
  198.3 1.9 copy-start.24
  199.2 0.6 copy-start.9
  200.3 1.9 collective-permute-start.2
  248.2 3.3 collective-permute-start.3
  251.5 3.7 copy-start.10
  254.3 1.3 copy-start.20
  255.2 9.7 %copy-start.11 = (f32[16,1024]{1,0:T(8,128)}, f32[16,1024]{1,0:T(8,128)S(1)}, u32[]{:S(2)}) copy-start(f32[16,1024]{1,0:T(8,128)S(1)} %add.126) | copy-start | bytes 196612
  255.7 1.8 collective-permute-start.4
  305.0 3.5 collective-permute-start.5
  308.4 3.7 copy-start.12
  311.2 1.3 copy-start.21
  312.1 9.7 %copy-start.13 = (f32[16,1024]{1,0:T(8,128)}, f32[16,1024]{1,0:T(8,128)S(1)}, u32[]{:S(2)}) copy-start(f32[16,1024]{1,0:T(8,128)S(1)} %add.129) | copy-start | bytes 196612
  312.6 1.7 collective-permute-start.6
  361.9 3.2 collective-permute-start.7
  365.2 3.7 copy-start.14
  368.0 1.3 copy-start.22
  368.8 9.7 %copy-start.15 = (f32[16,1024]{1,0:T(8,128)}, f32[16,1024]{1,0:T(8,128)S(1)}, u32[]{:S(2)}) copy-start(f32[16,1024]{1,0:T(8,128)S(1)} %add.132) | copy-start | bytes 196612
  369.3 1.8 collective-permute-start.8
  419.1 3.3 collective-permute-start.9
  422.3 3.7 copy-start.16
  425.1 1.9 copy-start.23
  426.0 0.6 copy-start.7
  427.1 1.8 collective-permute-start.10
  474.9 3.3 collective-permute-start.11
  478.2 3.7 copy-start.8
  481.0 1.3 copy-start.19
  482.4 1.8 collective-permute-start.12
  484.4 32.8 %copy-start.17 = (f32[8,2,512]{2,0,1:T(8,128)S(1)}, f32[8,2,512]{2,0,1:T(8,128)}, u32[]{:S(2)}) copy-start(f32[8,2,512]{2,0,1:T(8,128)} %get-tuple-element.5) | copy-start | bytes 98308
  516.3 14.5 %copy-start.5 = (bf16[384,1024]{1,0:T(8,128)(2,1)S(1)}, bf16[384,1024]{1,0:T(8,128)(2,1)}, u32[]{:S(2)}) copy-start(bf16[384,1024]{1,0:T(8,128)(2,1)} %copy-done.4) | copy-start | bytes 2359300
  517.1 1.4 collective-permute-start.13
Sparse Core Ops, SparseCore 0:
  9.2 44.7 all-gather.3
  56.4 23.1 reduce-scatter.1
  82.1 63.5 all-reduce.1
where the time goes:
time: 549 us; the launch traced here: 539 us
  blocking collectives  202 us (37%)
  waiting for transfers between devices  138 us (25%)
  local copies, waits for them, and re-layouts  74.1 us (13%)
  other arithmetic  67.5 us (12%)
  between operations  25.5 us (5%)
  starting transfers between devices  19.5 us (4%)
  matrix products  12.7 us (2%)
    all_to_all x6, blocking collectives, share_slots(): pieces = lax.all_to_all(mine, 'zx', 0, 0, tiled=True)  90.9 us
    all_to_all x6, blocking collectives, share_slots(): gathered = lax.all_to_all(spread, 'zx', 0, 0, tiled=True).reshape(-1)  85.7 us
    psum x1, waiting for transfers between devices, local(): coupling = lax.psum(partial_map.astype(jnp.bfloat16), 'sub')  66.1 us
    all_gather x1, waiting for transfers between devices, local(): lax.all_gather(disagg_rows, 'sub', axis=0, tiled=True)  32.1 us
    unnamed x87, local copies, waits for them, and re-layouts  26 us
    reduce_scatter x1, waiting for transfers between devices, local(): lax.psum_scatter(lax.dot_general(solved_half, agg_columns, CONTRACT_FIRST...  16.4 us
    all_to_all x7, other arithmetic, share_slots(): pieces = lax.all_to_all(mine, 'zx', 0, 0, tiled=True)  15.7 us
    broadcast_in_dim x7, other arithmetic, share_slots(): spread = jnp.broadcast_to(total, (chips, total.shape[1]))  13.8 us
  transfers between devices with their start and end apart: 19, of which 13 were waited for; matrix products, arithmetic and copies ran while one was open for 5% of the time, Pallas kernels for 0%

commit v1 on v0

--- a/solution.py
+++ b/solution.py
@@ -79,7 +79,7 @@
     partial_map = lax.dot_general(
         spread_half, agg_columns, CONTRACT_FIRST, preferred_element_type=jnp.float32
     )
-    coupling = lax.psum(partial_map.astype(jnp.bfloat16), "sub")
+    coupling = jnp.sum(lax.all_gather(partial_map.astype(jnp.bfloat16), "sub"), axis=0)
     domains = sweep_order.shape[0]
     members = domains // SEGMENTS
     segment_of = sweep_order * SEGMENTS // domains

time: 549 us -> 572 us (1.042)
  waiting for transfers between devices: 138 us -> 155 us
  other arithmetic: 67.5 us -> 76.7 us
    all_gather x0 -> x1, waiting for transfers between devices: none -> 68.8 us  [local(): lax.all_gather(partial_map.astype(jnp.bfloat16), 'sub')]
    psum x1 -> x0, waiting for transfers between devices: 66.1 us -> none  [local(): coupling = lax.psum(partial_map.astype(jnp.bfloat16), 'sub')]
    all_gather x1, waiting for transfers between devices: 32.1 us -> 46.6 us  [local(): lax.all_gather(disagg_rows, 'sub', axis=0, tiled=True)]
    reduce_sum x0 -> x1, other arithmetic: none -> 6.5 us  [local(): jnp.sum(lax.all_gather(partial_map.astype(jnp.bfloat16), 'sub'), axis=0)]
    unnamed x87 -> x79, local copies, waits for them, and re-layouts: 26 us -> 25.5 us
  transfers between devices with their start and end apart: 19 -> 19, of which waited for: 13 -> 15; matrix products, arithmetic and copies ran while one was open for 5% -> 5% of each run, Pallas kernels for 0% -> 0%
where the time goes in v1:
time: 572 us; the launch traced here: 561 us
  blocking collectives  200 us (35%)
  waiting for transfers between devices  155 us (27%)
  other arithmetic  76.7 us (13%)
  local copies, waits for them, and re-layouts  69.3 us (12%)
  between operations  25.6 us (4%)
  starting transfers between devices  21.3 us (4%)
  matrix products  12 us (2%)
    all_to_all x6, blocking collectives, share_slots(): pieces = lax.all_to_all(mine, 'zx', 0, 0, tiled=True)  90.8 us
    all_to_all x6, blocking collectives, share_slots(): gathered = lax.all_to_all(spread, 'zx', 0, 0, tiled=True).reshape(-1)  85.3 us
    all_gather x1, waiting for transfers between devices, local(): lax.all_gather(partial_map.astype(jnp.bfloat16), 'sub')  68.8 us
    all_gather x1, waiting for transfers between devices, local(): lax.all_gather(disagg_rows, 'sub', axis=0, tiled=True)  46.6 us
    unnamed x79, local copies, waits for them, and re-layouts  25.5 us
    reduce_scatter x1, waiting for transfers between devices, local(): lax.psum_scatter(lax.dot_general(solved_half, agg_columns, CONTRACT_FIRST...  20 us
    broadcast_in_dim x7, other arithmetic, share_slots(): spread = jnp.broadcast_to(total, (chips, total.shape[1]))  14.8 us
    all_to_all x7, other arithmetic, share_slots(): pieces = lax.all_to_all(mine, 'zx', 0, 0, tiled=True)  14.8 us
  transfers between devices with their start and end apart: 19, of which 15 were waited for; matrix products, arithmetic and copies ran while one was open for 5% of the time, Pallas kernels for 0%

profile of v1, /device:TPU:32, one launch (start us, length us, event | category | flops | bytes accessed | tf_op | source)
XLA Modules:
  0.0 560.7 jit_solution(3299740231663239707)
XLA Ops:
  7.3 46.6 %all-gather.6.cloned.1.call-done = bf16[1,1536,1024]{2,1,0:T(8,128)(2,1)} async-done(((bf16[1,384,1024]{2,1,0:T(8,128)(2,1)}), bf16[1,1536,1024]{2,1,0:T(8,128)(2,1)}) %all-gather.6.cloned.1.call-update) | async-done | bytes 3145744 | tf_op jit(solution)/shard_map/all_gather | solution.py:77
  53.9 3.3 fusion.2
  57.3 2.7 convolution_convert_fusion
  60.1 12.2 %all-gather = bf16[1,1536,64]{1,2,0:T(8,128)(2,1)S(1)} all-gather(bf16[1,384,64]{1,2,0:T(8,128)(2,1)S(1)} %copy-done.15), channel_id=2, replica_groups=mesh['zx'=32,'core'=2,'sub'=4] {'sub'}, dimensions={1}, use_global_device_ids=true | all-gather | bytes 245760 | tf_op jit(solution)/shard_map/all_gather | solution.py:67
  77.2 68.8 %all-gather.8.cloned.1.call-done = bf16[4096,1024]{1,0:T(8,128)(2,1)} async-done(((bf16[1024,1024]{1,0:T(8,128)(2,1)}), bf16[4096,1024]{1,0:T(8,128)(2,1)}) %all-gather.8.cloned.1.call-update) | async-done | bytes 8388624 | tf_op jit(solution)/shard_map/all_gather | solution.py:82
  146.0 6.5 %reduce_sum.223 = bf16[1024,1024]{1,0:T(8,128)(2,1)S(1)} reduce(bf16[4,1024,1024]{2,1,0:T(8,128)(2,1)} %bitcast.102, bf16[]{:T(256)} %constant.104.clone.1), dimensions={0}, to_apply=%region_2.3 | reduce | flops 3145728 | bytes 10485762 | tf_op jit(solution)/shard_map/reduce_sum | solution.py:82
  152.5 20.0 %reduce-scatter.2.cloned.1.call-done = bf16[16,1024]{1,0:T(8,128)(2,1)} async-done(((bf16[64,1024]{1,0:T(8,128)(2,1)}), bf16[16,1024]{1,0:T(8,128)(2,1)}) %reduce-scatter.2.cloned.1.call-update) | async-done | bytes 32784 | tf_op jit(solution)/shard_map/reduce_scatter | solution.py:69
  179.8 2.0 reduce.29
  181.8 1.6 reshape.729
  183.4 10.1 %all-to-all-start = ((bf16[32,2,1024]{2,1,0:T(2,128)(2,1)}), bf16[32,2,1024]{2,1,0:T(2,128)(2,1)}, u32[]{:S(2)}, u32[]{:S(2)}) async-start(bf16[32,2,1024]{2,1,0:T(2,128)(2,1)} %reshape.729), calls=%async_computation.1 | async-start | bytes 262144 | tf_op jit(solution)/shard_map/all_to_all | solution.py:35
  200.7 2.7 all-to-all-done
  203.4 1.4 reshape.730
  205.2 2.0 reduce.30
  207.2 1.6 reshape.731
  208.8 7.4 %all-to-all-start.1 = ((bf16[32,2,1024]{2,1,0:T(2,128)(2,1)}), bf16[32,2,1024]{2,1,0:T(2,128)(2,1)S(1)}, u32[]{:S(2)}, u32[]{:S(2)}) async-start(bf16[32,2,1024]{2,1,0:T(2,128)(2,1)} %reshape.731), calls=%async_computation.2 | async-start | bytes 262144 | tf_op jit(solution)/shard_map/all_to_all | solution.py:38
  217.0 1.6 select_reduce_fusion
  218.6 7.0 %all-to-all-done.1 = bf16[32,2,1024]{2,1,0:T(2,128)(2,1)S(1)} async-done(((bf16[32,2,1024]{2,1,0:T(2,128)(2,1)}), bf16[32,2,1024]{2,1,0:T(2,128)(2,1)S(1)}, u32[]{:S(2)}, u32[]{:S(2)}) %all-to-all-start.1) | async-done | bytes 131104 | tf_op jit(solution)/shard_map/all_to_all | solution.py:38
  226.4 1.7 reduce.15
  233.4 1.3 collective-permute-done.2
  235.5 1.8 reshape.692
  237.3 1.9 constant_dynamic-slice_fusion.5
  239.2 2.3 reduce.31
  242.3 15.1 %all_to_all.105 = bf16[32,2,1024]{2,1,0:T(2,128)(2,1)S(1)} all-to-all(bf16[32,2,1024]{2,1,0:T(2,128)(2,1)} %reshape.733), channel_id=1, replica_groups=mesh['zx'=32,'core'=2,'sub'=4] {'zx'}, dimensions={0} | all-to-all | bytes 262144 | tf_op jit(solution)/shard_map/all_to_all | solution.py:35
  260.2 2.3 reduce.32
  263.2 14.3 %all_to_all.106 = bf16[32,2,1024]{2,1,0:T(2,128)(2,1)S(1)} all-to-all(bf16[32,2,1024]{2,1,0:T(2,128)(2,1)} %reshape.735), channel_id=1, replica_groups=mesh['zx'=32,'core'=2,'sub'=4] {'zx'}, dimensions={0} | all-to-all | bytes 262144 | tf_op jit(solution)/shard_map/all_to_all | solution.py:38
  278.3 1.7 reduce.17
  280.7 1.3 slice_bitcast_fusion.11
  289.8 1.8 reshape.694
  291.7 1.9 constant_dynamic-slice_fusion.4
  293.6 2.3 reduce.33
  296.6 15.5 %all_to_all.107 = bf16[32,2,1024]{2,1,0:T(2,128)(2,1)S(1)} all-to-all(bf16[32,2,1024]{2,1,0:T(2,128)(2,1)} %reshape.737), channel_id=1, replica_groups=mesh['zx'=32,'core'=2,'sub'=4] {'zx'}, dimensions={0} | all-to-all | bytes 262144 | tf_op jit(solution)/shard_map/all_to_all | solution.py:35
  314.9 2.3 reduce.34
  317.9 14.3 %all_to_all.108 = bf16[32,2,1024]{2,1,0:T(2,128)(2,1)S(1)} all-to-all(bf16[32,2,1024]{2,1,0:T(2,128)(2,1)} %reshape.739), channel_id=1, replica_groups=mesh['zx'=32,'core'=2,'sub'=4] {'zx'}, dimensions={0} | all-to-all | bytes 262144 | tf_op jit(solution)/shard_map/all_to_all | solution.py:38
  333.0 1.7 reduce.19
  335.4 1.3 slice_bitcast_fusion.9
  344.6 1.8 reshape.696
  346.4 1.9 constant_dynamic-slice_fusion.3
  348.3 2.3 reduce.35
  351.3 15.3 %all_to_all.109 = bf16[32,2,1024]{2,1,0:T(2,128)(2,1)S(1)} all-to-all(bf16[32,2,1024]{2,1,0:T(2,128)(2,1)} %reshape.741), channel_id=1, replica_groups=mesh['zx'=32,'core'=2,'sub'=4] {'zx'}, dimensions={0} | all-to-all | bytes 262144 | tf_op jit(solution)/shard_map/all_to_all | solution.py:35
  369.4 2.3 reduce.36
  372.4 14.3 %all_to_all.110 = bf16[32,2,1024]{2,1,0:T(2,128)(2,1)S(1)} all-to-all(bf16[32,2,1024]{2,1,0:T(2,128)(2,1)} %reshape.743), channel_id=1, replica_groups=mesh['zx'=32,'core'=2,'sub'=4] {'zx'}, dimensions={0} | all-to-all | bytes 262144 | tf_op jit(solution)/shard_map/all_to_all | solution.py:38
  387.6 1.7 reduce.21
  389.9 1.3 slice_bitcast_fusion.7
  399.5 1.8 reshape.698
  401.4 1.9 constant_dynamic-slice_fusion.2
  403.3 2.3 reduce.37
  406.3 15.4 %all_to_all.111 = bf16[32,2,1024]{2,1,0:T(2,128)(2,1)S(1)} all-to-all(bf16[32,2,1024]{2,1,0:T(2,128)(2,1)} %reshape.745), channel_id=1, replica_groups=mesh['zx'=32,'core'=2,'sub'=4] {'zx'}, dimensions={0} | all-to-all | bytes 262144 | tf_op jit(solution)/shard_map/all_to_all | solution.py:35
  424.5 2.3 reduce.38
  427.5 14.3 %all_to_all.112 = bf16[32,2,1024]{2,1,0:T(2,128)(2,1)S(1)} all-to-all(bf16[32,2,1024]{2,1,0:T(2,128)(2,1)} %reshape.747), channel_id=1, replica_groups=mesh['zx'=32,'core'=2,'sub'=4] {'zx'}, dimensions={0} | all-to-all | bytes 262144 | tf_op jit(solution)/shard_map/all_to_all | solution.py:38
  442.7 1.7 reduce.23
  450.5 1.3 collective-permute-done.10
  452.6 1.8 reshape.700
  454.4 1.9 constant_dynamic-slice_fusion.1
  456.3 2.3 reduce.39
  459.3 15.2 %all_to_all.113 = bf16[32,2,1024]{2,1,0:T(2,128)(2,1)S(1)} all-to-all(bf16[32,2,1024]{2,1,0:T(2,128)(2,1)} %reshape.749), channel_id=1, replica_groups=mesh['zx'=32,'core'=2,'sub'=4] {'zx'}, dimensions={0} | all-to-all | bytes 262144 | tf_op jit(solution)/shard_map/all_to_all | solution.py:35
  477.3 2.3 reduce.40
  480.3 14.3 %all_to_all.114 = bf16[32,2,1024]{2,1,0:T(2,128)(2,1)S(1)} all-to-all(bf16[32,2,1024]{2,1,0:T(2,128)(2,1)} %reshape.751), channel_id=1, replica_groups=mesh['zx'=32,'core'=2,'sub'=4] {'zx'}, dimensions={0} | all-to-all | bytes 262144 | tf_op jit(solution)/shard_map/all_to_all | solution.py:38
  495.4 1.7 reduce.25
  497.9 1.3 slice_bitcast_fusion.3
  506.9 1.4 reduce.41
  508.3 14.4 %all_to_all.115 = bf16[32,2,1024]{2,1,0:T(2,128)(2,1)S(1)} all-to-all(bf16[32,2,1024]{2,1,0:T(2,128)(2,1)S(1)} %reshape.753), channel_id=1, replica_groups=mesh['zx'=32,'core'=2,'sub'=4] {'zx'}, dimensions={0} | all-to-all | bytes 262144 | tf_op jit(solution)/shard_map/all_to_all | solution.py:35
  523.2 1.4 reduce.42
  524.6 13.7 %all_to_all.116 = bf16[32,2,1024]{2,1,0:T(2,128)(2,1)S(1)} all-to-all(bf16[32,2,1024]{2,1,0:T(2,128)(2,1)S(1)} %reshape.755), channel_id=1, replica_groups=mesh['zx'=32,'core'=2,'sub'=4] {'zx'}, dimensions={0} | all-to-all | bytes 262144 | tf_op jit(solution)/shard_map/all_to_all | solution.py:38
  540.9 12.0 %all_gather.19 = bf16[64,1024]{1,0:T(8,128)(2,1)S(1)} all-gather(bf16[16,1024]{1,0:T(8,128)(2,1)S(1)} %add_convert_fusion), channel_id=1, replica_groups=mesh['zx'=32,'core'=2,'sub'=4] {'sub'}, dimensions={0}, use_global_device_ids=true | all-gather | bytes 163840 | tf_op jit(solution)/shard_map/all_gather | solution.py:114
  (213 shorter events, 86.9 us)
Async XLA Ops:
  6.5 47.4 %copy-start = (bf16[1,384,1536]{2,1,0:T(8,128)(2,1)S(1)}, bf16[1,384,1536]{2,1,0:T(8,128)(2,1)}, u32[]{:S(2)}) copy-start(bf16[1,384,1536]{2,1,0:T(8,128)(2,1)} %param.9) | copy-start | bytes 3538948
  6.5 47.4 %all-gather.6.cloned.1.call-start = ((), (), s32[]{:S(2)}) async-start(), calls=%async_computation.16 | async-start | bytes 3932160 | tf_op jit(solution)/shard_map/all_gather | solution.py:77
  7.3 50.0 %copy-start.7 = (bf16[1,1024,384]{2,1,0:T(8,128)(2,1)S(1)}, bf16[1,1024,384]{2,1,0:T(8,128)(2,1)}, u32[]{:S(2)}) copy-start(bf16[1,1024,384]{2,1,0:T(8,128)(2,1)} %param.10) | copy-start | bytes 2359300
  7.3 138.8 %all-gather.8.cloned.1.call-start = ((), (), s32[]{:S(2)}) async-start(), calls=%async_computation.17 | async-start | bytes 10485760 | tf_op jit(solution)/shard_map/all_gather | solution.py:82
  57.2 2.8 copy-start.5
  57.2 2.8 copy-start.15
  60.0 13.9 %copy-start.1 = (s32[64]{0:T(128)S(1)}, s32[64]{0:T(128)}, u32[]{:S(2)}) copy-start(s32[64]{0:T(128)} %param.15) | copy-start | bytes 772
  60.0 17.2 %copy-start.21 = (s32[1,6]{1,0:T(1,128)S(1)}, s32[1,6]{1,0:T(1,128)}, u32[]{:S(2)}) copy-start(s32[1,6]{1,0:T(1,128)} %param.13) | copy-start | bytes 76
  60.0 112.5 %reduce-scatter.2.cloned.1.call-start = ((), (), s32[]{:S(2)}) async-start(), calls=%async_computation.15 | async-start | bytes 163840 | tf_op jit(solution)/shard_map/reduce_scatter | solution.py:69
  72.8 73.3 %copy-start.3 = (f32[384,64]{0,1:T(8,128)}, f32[384,64]{0,1:T(8,128)S(1)}, u32[]{:S(2)}) copy-start(f32[384,64]{0,1:T(8,128)S(1)} %fusion.6) | copy-start | bytes 294916
  173.6 0.6 copy-start.13
  174.3 1.8 collective-permute-start
  175.6 23.9 %copy-start.20 = (s32[6]{0:T(128)}, s32[6]{0:T(128)S(1)}, u32[]{:S(2)}) copy-start(s32[6]{0:T(128)S(1)} %get-tuple-element.13) | copy-start | bytes 76
  183.4 20.1 %all-to-all-start = ((bf16[32,2,1024]{2,1,0:T(2,128)(2,1)}), bf16[32,2,1024]{2,1,0:T(2,128)(2,1)}, u32[]{:S(2)}, u32[]{:S(2)}) async-start(bf16[32,2,1024]{2,1,0:T(2,128)(2,1)} %reshape.729), calls=%async_computation.1 | async-start | bytes 262144 | tf_op jit(solution)/shard_map/all_to_all | solution.py:35
  208.8 16.8 %all-to-all-start.1 = ((bf16[32,2,1024]{2,1,0:T(2,128)(2,1)}), bf16[32,2,1024]{2,1,0:T(2,128)(2,1)S(1)}, u32[]{:S(2)}, u32[]{:S(2)}) async-start(bf16[32,2,1024]{2,1,0:T(2,128)(2,1)} %reshape.731), calls=%async_computation.2 | async-start | bytes 262144 | tf_op jit(solution)/shard_map/all_to_all | solution.py:38
  218.6 14.0 %copy-start.2 = (bf16[16,1024]{1,0:T(8,128)(2,1)S(1)}, bf16[16,1024]{1,0:T(8,128)(2,1)}, u32[]{:S(2)}) copy-start(bf16[16,1024]{1,0:T(8,128)(2,1)} %reduce-scatter.2.cloned.1.call-done) | copy-start | bytes 98308
  228.7 1.7 collective-permute-start.1
  233.1 1.6 collective-permute-start.2
  280.6 3.3 collective-permute-start.3
  285.9 1.3 copy-start.17
  286.8 9.1 %copy-start.8 = (f32[16,1024]{1,0:T(8,128)}, f32[16,1024]{1,0:T(8,128)S(1)}, u32[]{:S(2)}) copy-start(f32[16,1024]{1,0:T(8,128)S(1)} %add.124) | copy-start | bytes 196612
  287.3 1.8 collective-permute-start.4
  332.2 9.3 %copy-start.9 = (f32[16,1024]{1,0:T(8,128)S(1)}, f32[16,1024]{1,0:T(8,128)}, u32[]{:S(2)}) copy-start(f32[16,1024]{1,0:T(8,128)} %copy-done.8) | copy-start | bytes 196612
  335.4 3.3 collective-permute-start.5
  340.6 1.3 copy-start.18
  341.5 9.1 %copy-start.10 = (f32[16,1024]{1,0:T(8,128)}, f32[16,1024]{1,0:T(8,128)S(1)}, u32[]{:S(2)}) copy-start(f32[16,1024]{1,0:T(8,128)S(1)} %add.127) | copy-start | bytes 196612
  342.0 1.8 collective-permute-start.6
  386.8 9.3 %copy-start.11 = (f32[16,1024]{1,0:T(8,128)S(1)}, f32[16,1024]{1,0:T(8,128)}, u32[]{:S(2)}) copy-start(f32[16,1024]{1,0:T(8,128)} %copy-done.10) | copy-start | bytes 196612
  389.9 3.3 collective-permute-start.7
  395.2 1.3 copy-start.19
  396.1 9.5 %copy-start.12 = (f32[16,1024]{1,0:T(8,128)}, f32[16,1024]{1,0:T(8,128)S(1)}, u32[]{:S(2)}) copy-start(f32[16,1024]{1,0:T(8,128)S(1)} %add.130) | copy-start | bytes 196612
  396.6 2.2 collective-permute-start.8
  406.3 38.7 %copy-start.14 = (f32[8,2,512]{2,0,1:T(8,128)S(1)}, f32[8,2,512]{2,0,1:T(8,128)}, u32[]{:S(2)}) copy-start(f32[8,2,512]{2,0,1:T(8,128)} %get-tuple-element.9) | copy-start | bytes 98308
  445.0 1.7 collective-permute-start.9
  450.1 1.6 collective-permute-start.10
  497.8 3.4 collective-permute-start.11
  503.2 1.3 copy-start.16
  504.6 1.7 collective-permute-start.12
  538.5 14.5 %copy-start.4 = (f32[384,64]{0,1:T(8,128)S(1)}, f32[384,64]{0,1:T(8,128)}, u32[]{:S(2)}) copy-start(f32[384,64]{0,1:T(8,128)} %copy-done.3) | copy-start | bytes 294916
  538.5 14.5 %copy-start.6 = (bf16[384,1024]{1,0:T(8,128)(2,1)S(1)}, bf16[384,1024]{1,0:T(8,128)(2,1)}, u32[]{:S(2)}) copy-start(bf16[384,1024]{1,0:T(8,128)(2,1)} %copy-done.5) | copy-start | bytes 2359300
  539.2 1.4 collective-permute-start.13
Sparse Core Ops, SparseCore 0:
  9.2 44.7 all-gather.5
  60.1 85.8 all-gather.7
  148.5 23.9 reduce-scatter.1
